TPU v7x, 128 devices: a whole 4x4x4 slice. The times are simulated.
128 devices in a mesh: pr: 8 (over z, core), pc: 16 (over y, x).
Axes of the slice: x: 4, y: 4, z: 4, core: 2. Of those that a mesh axis runs over, the one named last changes fastest.
Arguments:
- test_points: bfloat16 [131072, 512], P('pr'), may hold values from -15 to 15
- panel_points: bfloat16 [1024, 512], P('pc'), may hold values from -15 to 15
- factor_rows: float32 [1024, 32768], P('pc', 'pr'), may hold values from -0.03125 to 0.03125
- alpha_below: float32 [32768, 128], P(('pr', 'pc')), may hold values from -6 to 6
- targets: float32 [1024, 128], P('pc'), may hold values from -6 to 6
- inverse_block: float32 [1024, 1024], P('pc'), may hold values from -0.008 to 0.08, as said below
- predictions_in: float32 [131072, 128], P(('pr', 'pc')), may hold values from -6 to 6
Outputs:
- predictions: float32 [131072, 128], P(('pr', 'pc'))
Inputs may be any that keep to these rules, and one draw needn't show every extreme that they name: `inverse_block`: lower triangular with a positive diagonal.
All inputs are finite; a program needn't handle non-finite values.
Results may differ from a plain program's by a relative error of at most 0.0003.
Values may be sent and summed in bfloat16 or wider, within the bound.
No kernel may reach another device: no remote copies, remote signals or barrier semaphores. Data moves between devices by JAX's collectives and lax.ppermute only.
A program may use at most 128 MiB of HBM per device.

v0:
```python
import math
import jax
import jax.numpy as jnp
from jax import lax
from jax.sharding import PartitionSpec as P

LAYERS = 4
bias_var = 0.1
weight_var = 2.0


def arc_kernel(panel, test, test_norms):
    width = panel.shape[1]
    cross = jnp.dot(panel, test.T, preferred_element_type=jnp.float32) / width
    panel_var = jnp.einsum("pd,pd->p", panel, panel, preferred_element_type=jnp.float32) / width
    kern = bias_var + weight_var * cross
    panel_k = bias_var + weight_var * panel_var
    test_k = bias_var + weight_var * (test_norms / width)
    for level in range(LAYERS):
        spread = jnp.sqrt(panel_k[:, None] * test_k[None, :])
        cosine = kern / spread
        theta = jnp.arccos(cosine)
        kern = bias_var + weight_var / (2.0 * math.pi) * spread * (
            jnp.sqrt(1.0 - cosine * cosine) + (math.pi - theta) * cosine
        )
        panel_k = bias_var + 0.5 * weight_var * panel_k
        test_k = bias_var + 0.5 * weight_var * test_k
    return kern


def contract_rows(left, right):
    return lax.dot_general(
        left,
        right,
        (((0,), (0,)), ((), ())),
        precision=lax.Precision.HIGHEST,
        preferred_element_type=jnp.float32,
    )


def body(
    test_points, panel_points, factor_rows, alpha_below, targets, inverse_block, predictions_in
):
    rows = predictions_in.shape[0]
    own = lax.axis_index("pc")
    partial_sum = jnp.dot(
        factor_rows,
        lax.all_gather(alpha_below, "pc", axis=0, tiled=True),
        precision=lax.Precision.HIGHEST,
        preferred_element_type=jnp.float32,
    )
    carried = lax.psum(partial_sum, "pr")
    residual = targets - carried
    alpha_panel = lax.psum(contract_rows(inverse_block, residual), "pc")
    panel_all = lax.all_gather(panel_points, "pc", axis=0, tiled=True)
    test_own = lax.dynamic_slice_in_dim(test_points, own * rows, rows, 0)
    test_norms = jnp.einsum("nd,nd->n", test_own, test_own, preferred_element_type=jnp.float32)
    kern = lax.optimization_barrier(arc_kernel(panel_all, test_own, test_norms))
    update = contract_rows(kern, alpha_panel)
    return predictions_in + update


def solution(mesh):
    placed = (
        P("pr", None),
        P("pc", None),
        P("pc", "pr"),
        P(("pr", "pc"), None),
        P("pc", None),
        P("pc", None),
        P(("pr", "pc"), None),
    )
    return jax.shard_map(
        body, mesh=mesh, in_specs=placed, out_specs=P(("pr", "pc"), None), check_vma=False
    )
```

profile of v0, /device:TPU:0, one launch (start us, length us, event | category | flops | bytes accessed | tf_op | source)
XLA Modules:
  0.0 224.8 jit_solution(2418785735525503081)
XLA Ops:
  6.5 0.0 copy-start
  6.5 0.0 copy-start.3
  6.5 0.0 copy-start.4
  6.5 0.0 all-gather.3.cloned.1.call-start
  6.5 0.7 all-gather.3.cloned.1.call-update
  7.3 0.0 all-gather.5.cloned.1.call-start
  7.3 0.7 all-gather.5.cloned.1.call-update
  8.0 0.0 all-reduce.2.cloned.1.call-start
  8.1 1.5 fusion
  9.6 44.7 %all-gather.3.cloned.1.call-done = bf16[1024,512]{1,0:T(8,128)(2,1)} async-done(((bf16[64,512]{1,0:T(8,128)(2,1)}), bf16[1024,512]{1,0:T(8,128)(2,1)}) %all-gather.3.cloned.1.call-update) | async-done | bytes 1048592 | tf_op jit(solution)/shard_map/all_gather | solution.py:55
  54.3 0.0 copy-start.1
  54.3 1.6 fusion.1
  55.9 44.7 %all-gather.5.cloned.1.call-done = f32[4096,128]{1,0:T(8,128)} async-done(((f32[256,128]{1,0:T(8,128)}), f32[4096,128]{1,0:T(8,128)}) %all-gather.5.cloned.1.call-update) | async-done | bytes 2097168 | tf_op jit(solution)/shard_map/all_gather | solution.py:48
  100.6 0.0 copy-done
  100.6 3.0 %fusion.5 = f32[64,128]{1,0:T(8,128)S(1)} fusion(f32[64,4096]{1,0:T(8,128)S(1)} %copy-done, f32[4096,128]{1,0:T(8,128)} %all-gather.5.cloned.1.call-done), kind=kOutput, calls=%fused_computation.19 | convolution fusion | flops 402653184 | bytes 3178496 | tf_op jit(solution)/shard_map/dot_general | solution.py:46
  103.6 24.3 %psum.14 = f32[64,128]{1,0:T(8,128)S(1)} all-reduce(f32[64,128]{1,0:T(8,128)S(1)} %fusion.5), channel_id=1, replica_groups=mesh['pr'=8,'pc'=16] {'pr'}, use_global_device_ids=true, to_apply=%region_0.0 | all-reduce | flops 8192 | bytes 65536 | tf_op jit(solution)/shard_map/psum | solution.py:52
  127.9 0.0 copy-done.3
  127.9 0.0 copy-done.4
  127.9 1.4 convolution_bitcast_fusion
  129.3 0.0 all-reduce.2.cloned.1.call-update
  129.3 0.0 copy-done.1
  129.4 0.0 copy-start.2
  129.4 50.0 %multiply_add_fusion = f32[1024,1024]{0,1:T(8,128)} fusion(bf16[1024,512]{1,0:T(8,128)(2,1)S(1)} %copy-done.1, f32[1024]{0:T(1024)S(1)} %get-tuple-element.12, f32[1024]{0:T(1024)S(1)} %get-tuple-element.8, f32[1024]{0:T(1024)S(1)} %get-tuple-element.11, f32[1024]{0:T(1024)S(1)} %get-tuple-element.7, f32[1024]{0:T(1024)S(1)} %get-tuple-element.10, ...), kind=kOutput, calls=%fused_computation.1 | convolution fusion | flops 1130364928 | bytes 6324228 | tf_op jit(solution)/shard_map/dot_general | solution.py:14
  179.3 32.4 %all-reduce.2.cloned.1.call-done = f32[1024,128]{0,1:T(8,128)} async-done(((f32[1024,128]{0,1:T(8,128)}), f32[1024,128]{0,1:T(8,128)}) %all-reduce.2.cloned.1.call-update) | async-done | bytes 524304 | tf_op jit(solution)/shard_map/psum | solution.py:54
  211.7 0.0 copy-done.2
  211.7 6.5 %convolution_add_fusion = f32[1024,128]{1,0:T(8,128)} fusion(f32[1024,128]{1,0:T(8,128)S(1)} %copy-done.2, f32[1024,1024]{0,1:T(8,128)} %multiply_add_fusion, f32[1024,128]{0,1:T(8,128)} %all-reduce.2.cloned.1.call-done), kind=kOutput, calls=%fused_computation.6 | convolution fusion | flops 1610743808 | bytes 5767168 | tf_op jit(solution)/shard_map/dot_general | solution.py:32
  (2 shorter events, 0.0 us)
Async XLA Ops:
  6.5 94.1 %copy-start = (f32[64,4096]{1,0:T(8,128)S(1)}, f32[64,4096]{1,0:T(8,128)}, u32[]{:S(2)}) copy-start(f32[64,4096]{1,0:T(8,128)} %param.9) | copy-start | bytes 3145732
  6.5 121.4 %copy-start.3 = (f32[64,1024]{1,0:T(8,128)S(1)}, f32[64,1024]{1,0:T(8,128)}, u32[]{:S(2)}) copy-start(f32[64,1024]{1,0:T(8,128)} %param.12) | copy-start | bytes 786436
  6.5 121.4 %copy-start.4 = (f32[64,128]{1,0:T(8,128)S(1)}, f32[64,128]{1,0:T(8,128)}, u32[]{:S(2)}) copy-start(f32[64,128]{1,0:T(8,128)} %param.11) | copy-start | bytes 98308
  6.5 47.8 %all-gather.3.cloned.1.call-start = ((), (), s32[]{:S(2)}) async-start(), calls=%async_computation | async-start | bytes 1114112 | tf_op jit(solution)/shard_map/all_gather | solution.py:55
  7.3 93.4 %all-gather.5.cloned.1.call-start = ((), (), s32[]{:S(2)}) async-start(), calls=%async_computation.1 | async-start | bytes 2228224 | tf_op jit(solution)/shard_map/all_gather | solution.py:48
  8.0 203.7 %all-reduce.2.cloned.1.call-start = ((), (), s32[]{:S(2)}) async-start(), calls=%async_computation.2 | async-start | bytes 1048576 | tf_op jit(solution)/shard_map/psum | solution.py:54
  54.3 75.0 %copy-start.1 = (bf16[1024,512]{1,0:T(8,128)(2,1)S(1)}, bf16[1024,512]{1,0:T(8,128)(2,1)}, u32[]{:S(2)}) copy-start(bf16[1024,512]{1,0:T(8,128)(2,1)} %all-gather.3.cloned.1.call-done) | copy-start | bytes 3145732
  129.4 82.4 %copy-start.2 = (f32[1024,128]{1,0:T(8,128)S(1)}, f32[1024,128]{1,0:T(8,128)}, u32[]{:S(2)}) copy-start(f32[1024,128]{1,0:T(8,128)} %param.13) | copy-start | bytes 1572868
Sparse Core Ops, SparseCore 0:
  9.5 44.8 all-gather.2
  56.5 44.1 all-gather.4
  129.5 82.2 all-reduce.1
where the time goes:
time: 225 us
  waiting for transfers between devices  123 us (55%)
  matrix products  60.9 us (27%)
  blocking collectives  24.3 us (11%)
  between operations  13.2 us (6%)
  other arithmetic  3.1 us (1%)
    dot_general x1, matrix products, arc_kernel(): cross = jnp.dot(panel, test.T, preferred_element_type=jnp.float32) / width  50 us
    all_gather x1, waiting for transfers between devices, body(): panel_all = lax.all_gather(panel_points, 'pc', axis=0, tiled=True)  44.7 us
    all_gather x1, waiting for transfers between devices, body(): lax.all_gather(alpha_below, 'pc', axis=0, tiled=True)  44.7 us
    psum x1, waiting for transfers between devices, body(): alpha_panel = lax.psum(contract_rows(inverse_block, residual), 'pc')  32.4 us
    psum x1, blocking collectives, body(): carried = lax.psum(partial_sum, 'pr')  24.3 us
    dot_general x2, matrix products, contract_rows(): lax.dot_general(left, right, (((0,), (0,)), ((), ())), precision=lax.Prec...  7.94 us
  transfers between devices with their start and end apart: 3, of which 3 were waited for; matrix products, arithmetic and copies ran while one was open for 24% of the time, Pallas kernels for 0%

commit v1 on v0

--- a/solution.py
+++ b/solution.py
@@ -1,3 +1,4 @@
+import functools
 import math
 import jax
 import jax.numpy as jnp
@@ -7,6 +8,31 @@
 LAYERS = 4
 bias_var = 0.1
 weight_var = 2.0
+
+
+def mix_outputs_now(vals, d0):
+    extra, oldest, parts_out = (lax.axis_size("pc"), lax.axis_index("pc"), vals.shape[d0])
+    tmp = lax.dynamic_update_slice_in_dim(
+        jnp.zeros([t * extra if w == d0 else t for w, t in enumerate(vals.shape)], vals.dtype),
+        vals,
+        oldest * parts_out,
+        axis=d0,
+    )
+    arr_out = w1 = vals
+    for dd in range(1, extra // 2 + 1):
+        arr_out = lax.ppermute(arr_out, "pc", perm=[(w, (w + 1) % extra) for w in range(extra)])
+        tmp = lax.dynamic_update_slice_in_dim(
+            tmp, arr_out, (oldest - dd) % extra * parts_out, axis=d0
+        )
+        if 2 * dd < extra:
+            w1 = lax.ppermute(w1, "pc", [(w, (w - 1) % extra) for w in range(extra)])
+            tmp = lax.dynamic_update_slice_in_dim(
+                tmp, w1, (oldest + dd) % extra * parts_out, axis=d0
+            )
+    return tmp
+
+
+_remake_rails = functools.partial(mix_outputs_now, d0=0)
 
 
 def arc_kernel(panel, test, test_norms):
@@ -52,7 +78,7 @@
     carried = lax.psum(partial_sum, "pr")
     residual = targets - carried
     alpha_panel = lax.psum(contract_rows(inverse_block, residual), "pc")
-    panel_all = lax.all_gather(panel_points, "pc", axis=0, tiled=True)
+    panel_all = _remake_rails(panel_points)
     test_own = lax.dynamic_slice_in_dim(test_points, own * rows, rows, 0)
     test_norms = jnp.einsum("nd,nd->n", test_own, test_own, preferred_element_type=jnp.float32)
     kern = lax.optimization_barrier(arc_kernel(panel_all, test_own, test_norms))

time: 225 us -> 202 us (0.90)
  waiting for transfers between devices: 123 us -> 56.3 us
  starting transfers between devices: 0.08 us -> 39.5 us
  matrix products: 60.9 us -> 64.4 us
    all_gather x1 -> x0, waiting for transfers between devices: 44.7 us -> none  [body(): panel_all = lax.all_gather(panel_points, 'pc', axis=0, tiled=True)]
    all_gather x1, waiting for transfers between devices: 44.7 us -> 0.02 us  [body(): lax.all_gather(alpha_below, 'pc', axis=0, tiled=True)]
    ppermute x0 -> x15, starting transfers between devices: none -> 39.5 us  [the longest x7 39.4 us: mix_outputs_now(): w1 = lax.ppermute(w1, 'pc', [(w, (w - 1) % extra) for w in range(extra)])]
    ppermute x0 -> x15, waiting for transfers between devices: none -> 26.9 us  [the longest x8 20.3 us: mix_outputs_now(): lax.ppermute(arr_out, 'pc', perm=[(w, (w + 1) % extra) for w in range(ext...]
    psum x1, waiting for transfers between devices: 32.4 us -> 28.7 us  [body(): alpha_panel = lax.psum(contract_rows(inverse_block, residual), 'pc')]
    dot_general x2, matrix products: 7.94 us -> 11.2 us  [contract_rows(): lax.dot_general(left, right, (((0,), (0,)), ((), ())), precision=lax.Prec...]
  transfers between devices with their start and end apart: 3 -> 17, of which waited for: 3 -> 13; matrix products, arithmetic and copies ran while one was open for 24% -> 26% of each run, Pallas kernels for 0% -> 0%
where the time goes in v1:
time: 202 us; the launch traced here: 201 us
  matrix products  64.4 us (32%)
  waiting for transfers between devices  56.3 us (28%)
  starting transfers between devices  39.5 us (20%)
  blocking collectives  24.7 us (12%)
  between operations  13.6 us (7%)
    dot_general x1, matrix products, arc_kernel(): cross = jnp.dot(panel, test.T, preferred_element_type=jnp.float32) / width  50.3 us
    ppermute x7, starting transfers between devices, mix_outputs_now(): w1 = lax.ppermute(w1, 'pc', [(w, (w - 1) % extra) for w in range(extra)])  39.4 us
    psum x1, waiting for transfers between devices, body(): alpha_panel = lax.psum(contract_rows(inverse_block, residual), 'pc')  28.7 us
    psum x1, blocking collectives, body(): carried = lax.psum(partial_sum, 'pr')  24.7 us
    ppermute x8, waiting for transfers between devices, mix_outputs_now(): lax.ppermute(arr_out, 'pc', perm=[(w, (w + 1) % extra) for w in range(ext...  20.3 us
    dot_general x2, matrix products, contract_rows(): lax.dot_general(left, right, (((0,), (0,)), ((), ())), precision=lax.Prec...  11.2 us
    ppermute x7, waiting for transfers between devices, mix_outputs_now(): w1 = lax.ppermute(w1, 'pc', [(w, (w - 1) % extra) for w in range(extra)])  6.62 us
  transfers between devices with their start and end apart: 17, of which 13 were waited for; matrix products, arithmetic and copies ran while one was open for 26% of the time, Pallas kernels for 0%

profile of v1, /device:TPU:0, one launch (start us, length us, event | category | flops | bytes accessed | tf_op | source)
XLA Modules:
  0.0 201.4 jit_solution(9588055798101494730)
XLA Ops:
  6.5 0.0 copy-start
  6.5 0.0 all-gather.2.cloned.1.call-start
  6.5 0.7 all-gather.2.cloned.1.call-update
  7.3 0.0 all-reduce.2.cloned.1.call-start
  7.3 5.4 %collective-permute-start.1 = (bf16[64,512]{1,0:T(8,128)(2,1)}, bf16[64,512]{1,0:T(8,128)(2,1)S(1)}, u32[]{:S(2)}, u32[]{:S(2)}) collective-permute-start(bf16[64,512]{1,0:T(8,128)(2,1)} %param.8), channel_id=1, source_target_pairs={{0,15},{1,0},{2,1},{3,2},{4,3},{5,4},{6,5},{7,6},{8,7},{9,8},{10,9... | collective-permute-start | bytes 196616 | tf_op jit(solution)/shard_map/ppermute | solution.py:28
  12.7 0.0 collective-permute-start
  12.7 1.5 fusion
  14.3 0.1 broadcast_in_dim.2
  14.3 0.9 constant_dynamic-update-slice_fusion.15
  15.2 0.0 collective-permute-done.1
  15.2 5.4 %collective-permute-start.3 = (bf16[64,512]{1,0:T(8,128)(2,1)S(1)}, bf16[64,512]{1,0:T(8,128)(2,1)S(1)}, u32[]{:S(2)}, u32[]{:S(2)}) collective-permute-start(bf16[64,512]{1,0:T(8,128)(2,1)S(1)} %collective-permute-done.1), channel_id=1, source_target_pairs={{0,15},{1,0},{2,1},{3,2},{4,3},{5,4},{6,5},{7,6},{8,7},{9,8},{10,9... | collective-permute-start | bytes 196616 | tf_op jit(solution)/shard_map/ppermute | solution.py:28
  20.6 0.0 collective-permute-done
  20.6 0.0 collective-permute-start.2
  20.6 1.9 collective-permute-done.3
  22.5 5.7 %collective-permute-start.5 = (bf16[64,512]{1,0:T(8,128)(2,1)S(1)}, bf16[64,512]{1,0:T(8,128)(2,1)S(1)}, u32[]{:S(2)}, u32[]{:S(2)}) collective-permute-start(bf16[64,512]{1,0:T(8,128)(2,1)S(1)} %collective-permute-done.3), channel_id=1, source_target_pairs={{0,15},{1,0},{2,1},{3,2},{4,3},{5,4},{6,5},{7,6},{8,7},{9,8},{10,9... | collective-permute-start | bytes 196616 | tf_op jit(solution)/shard_map/ppermute | solution.py:28
  28.2 0.5 collective-permute-done.2
  28.7 0.0 collective-permute-start.4
  28.7 1.4 collective-permute-done.5
  30.1 5.7 %collective-permute-start.7 = (bf16[64,512]{1,0:T(8,128)(2,1)S(1)}, bf16[64,512]{1,0:T(8,128)(2,1)S(1)}, u32[]{:S(2)}, u32[]{:S(2)}) collective-permute-start(bf16[64,512]{1,0:T(8,128)(2,1)S(1)} %collective-permute-done.5), channel_id=1, source_target_pairs={{0,15},{1,0},{2,1},{3,2},{4,3},{5,4},{6,5},{7,6},{8,7},{9,8},{10,9... | collective-permute-start | bytes 196616 | tf_op jit(solution)/shard_map/ppermute | solution.py:28
  35.8 0.7 collective-permute-done.4
  36.5 0.0 collective-permute-start.6
  36.5 1.2 collective-permute-done.7
  37.7 5.7 %collective-permute-start.9 = (bf16[64,512]{1,0:T(8,128)(2,1)S(1)}, bf16[64,512]{1,0:T(8,128)(2,1)S(1)}, u32[]{:S(2)}, u32[]{:S(2)}) collective-permute-start(bf16[64,512]{1,0:T(8,128)(2,1)S(1)} %collective-permute-done.7), channel_id=1, source_target_pairs={{0,15},{1,0},{2,1},{3,2},{4,3},{5,4},{6,5},{7,6},{8,7},{9,8},{10,9... | collective-permute-start | bytes 196616 | tf_op jit(solution)/shard_map/ppermute | solution.py:28
  43.4 0.7 collective-permute-done.6
  44.1 0.0 collective-permute-start.8
  44.1 1.2 collective-permute-done.9
  45.3 5.8 %collective-permute-start.11 = (bf16[64,512]{1,0:T(8,128)(2,1)S(1)}, bf16[64,512]{1,0:T(8,128)(2,1)S(1)}, u32[]{:S(2)}, u32[]{:S(2)}) collective-permute-start(bf16[64,512]{1,0:T(8,128)(2,1)S(1)} %collective-permute-done.9), channel_id=1, source_target_pairs={{0,15},{1,0},{2,1},{3,2},{4,3},{5,4},{6,5},{7,6},{8,7},{9,8},{10,9... | collective-permute-start | bytes 196616 | tf_op jit(solution)/shard_map/ppermute | solution.py:28
  51.1 2.6 %collective-permute-done.8 = bf16[64,512]{1,0:T(8,128)(2,1)S(1)} collective-permute-done((bf16[64,512]{1,0:T(8,128)(2,1)S(1)}, bf16[64,512]{1,0:T(8,128)(2,1)S(1)}, u32[]{:S(2)}, u32[]{:S(2)}) %collective-permute-start.8) | collective-permute-done | bytes 65568 | tf_op jit(solution)/shard_map/ppermute | solution.py:23
  53.7 0.0 collective-permute-start.10
  53.7 1.1 collective-permute-done.11
  54.7 5.8 %collective-permute-start.13 = (bf16[64,512]{1,0:T(8,128)(2,1)S(1)}, bf16[64,512]{1,0:T(8,128)(2,1)S(1)}, u32[]{:S(2)}, u32[]{:S(2)}) collective-permute-start(bf16[64,512]{1,0:T(8,128)(2,1)S(1)} %collective-permute-done.11), channel_id=1, source_target_pairs={{0,15},{1,0},{2,1},{3,2},{4,3},{5,4},{6,5},{7,6},{8,7},{9,8},{10,9... | collective-permute-start | bytes 196616 | tf_op jit(solution)/shard_map/ppermute | solution.py:28
  60.5 0.7 collective-permute-done.10
  61.2 0.0 collective-permute-start.12
  61.3 7.6 %collective-permute-done.12 = bf16[64,512]{1,0:T(8,128)(2,1)S(1)} collective-permute-done((bf16[64,512]{1,0:T(8,128)(2,1)S(1)}, bf16[64,512]{1,0:T(8,128)(2,1)S(1)}, u32[]{:S(2)}, u32[]{:S(2)}) %collective-permute-start.12) | collective-permute-done | bytes 65568 | tf_op jit(solution)/shard_map/ppermute | solution.py:23
  68.8 0.0 collective-permute-start.14
  68.8 0.0 collective-permute-done.13
  68.9 7.5 %collective-permute-done.14 = bf16[64,512]{1,0:T(8,128)(2,1)S(1)} collective-permute-done((bf16[64,512]{1,0:T(8,128)(2,1)S(1)}, bf16[64,512]{1,0:T(8,128)(2,1)S(1)}, u32[]{:S(2)}, u32[]{:S(2)}) %collective-permute-start.14) | collective-permute-done | bytes 65568 | tf_op jit(solution)/shard_map/ppermute | solution.py:23
  76.4 0.3 fusion.1
  76.7 0.0 all-gather.2.cloned.1.call-done
  76.7 0.0 copy-done
  76.8 3.0 %fusion.5 = f32[64,128]{1,0:T(8,128)S(1)} fusion(f32[64,4096]{1,0:T(8,128)S(1)} %copy-done, f32[4096,128]{1,0:T(8,128)} %all-gather.2.cloned.1.call-done), kind=kOutput, calls=%fused_computation.34 | convolution fusion | flops 402653184 | bytes 3178496 | tf_op jit(solution)/shard_map/dot_general | solution.py:72
  79.7 24.7 %psum.14 = f32[64,128]{1,0:T(8,128)S(1)} all-reduce(f32[64,128]{1,0:T(8,128)S(1)} %fusion.5), channel_id=1, replica_groups=mesh['pr'=8,'pc'=16] {'pr'}, use_global_device_ids=true, to_apply=%region_0.0 | all-reduce | flops 8192 | bytes 65536 | tf_op jit(solution)/shard_map/psum | solution.py:78
  104.4 1.4 convolution_bitcast_fusion
  105.9 0.0 all-reduce.2.cloned.1.call-update
  105.9 0.0 copy-start.1
  105.9 50.3 %multiply_add_fusion = f32[1024,1024]{1,0:T(8,128)} fusion(bf16[1024,512]{1,0:T(8,128)(2,1)S(1)} %constant_dynamic-update-slice_fusion, f32[1024]{0:T(1024)S(1)} %get-tuple-element.12, f32[1024]{0:T(1024)S(1)} %get-tuple-element.8, f32[1024]{0:T(1024)S(1)} %get-tuple-element.11, f32[1024]{0:T(1024)S(1)} %get-tuple-element.7, f32[1024]{0:T(1024)S(1)} %get-tuple-element.10, ...), kind=kOutput, calls=%fused_computation | convolution fusion | flops 1130364928 | bytes 6324228 | tf_op jit(solution)/shard_map/dot_general | solution.py:40
  156.1 28.7 %all-reduce.2.cloned.1.call-done = f32[1024,128]{0,1:T(8,128)} async-done(((f32[1024,128]{0,1:T(8,128)}), f32[1024,128]{0,1:T(8,128)}) %all-reduce.2.cloned.1.call-update) | async-done | bytes 524304 | tf_op jit(solution)/shard_map/psum | solution.py:80
  184.8 9.8 %convolution_add_fusion = f32[1024,128]{1,0:T(8,128)} fusion(f32[1024,128]{1,0:T(8,128)S(1)} %copy-done.1, f32[1024,1024]{1,0:T(8,128)} %multiply_add_fusion, f32[1024,128]{0,1:T(8,128)} %all-reduce.2.cloned.1.call-done), kind=kOutput, calls=%fused_computation.5 | convolution fusion | flops 1610743808 | bytes 5767168 | tf_op jit(solution)/shard_map/dot_general | solution.py:58
  (22 shorter events, 0.2 us)
Async XLA Ops:
  6.5 70.2 %copy-start = (f32[64,4096]{1,0:T(8,128)S(1)}, f32[64,4096]{1,0:T(8,128)}, u32[]{:S(2)}) copy-start(f32[64,4096]{1,0:T(8,128)} %param.9) | copy-start | bytes 3145732
  6.5 70.2 %all-gather.2.cloned.1.call-start = ((), (), s32[]{:S(2)}) async-start(), calls=%async_computation | async-start | bytes 2228224 | tf_op jit(solution)/shard_map/all_gather | solution.py:74
  7.3 177.6 %all-reduce.2.cloned.1.call-start = ((), (), s32[]{:S(2)}) async-start(), calls=%async_computation.1 | async-start | bytes 1048576 | tf_op jit(solution)/shard_map/psum | solution.py:80
  7.3 7.9 %collective-permute-start.1 = (bf16[64,512]{1,0:T(8,128)(2,1)}, bf16[64,512]{1,0:T(8,128)(2,1)S(1)}, u32[]{:S(2)}, u32[]{:S(2)}) collective-permute-start(bf16[64,512]{1,0:T(8,128)(2,1)} %param.8), channel_id=1, source_target_pairs={{0,15},{1,0},{2,1},{3,2},{4,3},{5,4},{6,5},{7,6},{8,7},{9,8},{10,9... | collective-permute-start | bytes 196616 | tf_op jit(solution)/shard_map/ppermute | solution.py:28
  12.7 7.9 %collective-permute-start = (bf16[64,512]{1,0:T(8,128)(2,1)}, bf16[64,512]{1,0:T(8,128)(2,1)S(1)}, u32[]{:S(2)}, u32[]{:S(2)}) collective-permute-start(bf16[64,512]{1,0:T(8,128)(2,1)} %param.8), channel_id=1, source_target_pairs={{0,1},{1,2},{2,3},{3,4},{4,5},{5,6},{6,7},{7,8},{8,9},{9,10},{10,1... | collective-permute-start | bytes 196616 | tf_op jit(solution)/shard_map/ppermute | solution.py:23
  12.7 91.7 %copy-start.2 = (f32[64,1024]{1,0:T(8,128)S(1)}, f32[64,1024]{1,0:T(8,128)}, u32[]{:S(2)}) copy-start(f32[64,1024]{1,0:T(8,128)} %param.12) | copy-start | bytes 786436
  12.7 91.7 %copy-start.3 = (f32[64,128]{1,0:T(8,128)S(1)}, f32[64,128]{1,0:T(8,128)}, u32[]{:S(2)}) copy-start(f32[64,128]{1,0:T(8,128)} %param.11) | copy-start | bytes 98308
  15.2 7.3 %collective-permute-start.3 = (bf16[64,512]{1,0:T(8,128)(2,1)S(1)}, bf16[64,512]{1,0:T(8,128)(2,1)S(1)}, u32[]{:S(2)}, u32[]{:S(2)}) collective-permute-start(bf16[64,512]{1,0:T(8,128)(2,1)S(1)} %collective-permute-done.1), channel_id=1, source_target_pairs={{0,15},{1,0},{2,1},{3,2},{4,3},{5,4},{6,5},{7,6},{8,7},{9,8},{10,9... | collective-permute-start | bytes 196616 | tf_op jit(solution)/shard_map/ppermute | solution.py:28
  20.6 8.1 %collective-permute-start.2 = (bf16[64,512]{1,0:T(8,128)(2,1)S(1)}, bf16[64,512]{1,0:T(8,128)(2,1)S(1)}, u32[]{:S(2)}, u32[]{:S(2)}) collective-permute-start(bf16[64,512]{1,0:T(8,128)(2,1)S(1)} %collective-permute-done), channel_id=1, source_target_pairs={{0,1},{1,2},{2,3},{3,4},{4,5},{5,6},{6,7},{7,8},{8,9},{9,10},{10,1... | collective-permute-start | bytes 196616 | tf_op jit(solution)/shard_map/ppermute | solution.py:23
  22.5 7.6 %collective-permute-start.5 = (bf16[64,512]{1,0:T(8,128)(2,1)S(1)}, bf16[64,512]{1,0:T(8,128)(2,1)S(1)}, u32[]{:S(2)}, u32[]{:S(2)}) collective-permute-start(bf16[64,512]{1,0:T(8,128)(2,1)S(1)} %collective-permute-done.3), channel_id=1, source_target_pairs={{0,15},{1,0},{2,1},{3,2},{4,3},{5,4},{6,5},{7,6},{8,7},{9,8},{10,9... | collective-permute-start | bytes 196616 | tf_op jit(solution)/shard_map/ppermute | solution.py:28
  28.7 7.8 %collective-permute-start.4 = (bf16[64,512]{1,0:T(8,128)(2,1)S(1)}, bf16[64,512]{1,0:T(8,128)(2,1)S(1)}, u32[]{:S(2)}, u32[]{:S(2)}) collective-permute-start(bf16[64,512]{1,0:T(8,128)(2,1)S(1)} %collective-permute-done.2), channel_id=1, source_target_pairs={{0,1},{1,2},{2,3},{3,4},{4,5},{5,6},{6,7},{7,8},{8,9},{9,10},{10,1... | collective-permute-start | bytes 196616 | tf_op jit(solution)/shard_map/ppermute | solution.py:23
  30.1 7.6 %collective-permute-start.7 = (bf16[64,512]{1,0:T(8,128)(2,1)S(1)}, bf16[64,512]{1,0:T(8,128)(2,1)S(1)}, u32[]{:S(2)}, u32[]{:S(2)}) collective-permute-start(bf16[64,512]{1,0:T(8,128)(2,1)S(1)} %collective-permute-done.5), channel_id=1, source_target_pairs={{0,15},{1,0},{2,1},{3,2},{4,3},{5,4},{6,5},{7,6},{8,7},{9,8},{10,9... | collective-permute-start | bytes 196616 | tf_op jit(solution)/shard_map/ppermute | solution.py:28
  36.5 7.6 %collective-permute-start.6 = (bf16[64,512]{1,0:T(8,128)(2,1)S(1)}, bf16[64,512]{1,0:T(8,128)(2,1)S(1)}, u32[]{:S(2)}, u32[]{:S(2)}) collective-permute-start(bf16[64,512]{1,0:T(8,128)(2,1)S(1)} %collective-permute-done.4), channel_id=1, source_target_pairs={{0,1},{1,2},{2,3},{3,4},{4,5},{5,6},{6,7},{7,8},{8,9},{9,10},{10,1... | collective-permute-start | bytes 196616 | tf_op jit(solution)/shard_map/ppermute | solution.py:23
  37.7 7.6 %collective-permute-start.9 = (bf16[64,512]{1,0:T(8,128)(2,1)S(1)}, bf16[64,512]{1,0:T(8,128)(2,1)S(1)}, u32[]{:S(2)}, u32[]{:S(2)}) collective-permute-start(bf16[64,512]{1,0:T(8,128)(2,1)S(1)} %collective-permute-done.7), channel_id=1, source_target_pairs={{0,15},{1,0},{2,1},{3,2},{4,3},{5,4},{6,5},{7,6},{8,7},{9,8},{10,9... | collective-permute-start | bytes 196616 | tf_op jit(solution)/shard_map/ppermute | solution.py:28
  44.1 9.6 %collective-permute-start.8 = (bf16[64,512]{1,0:T(8,128)(2,1)S(1)}, bf16[64,512]{1,0:T(8,128)(2,1)S(1)}, u32[]{:S(2)}, u32[]{:S(2)}) collective-permute-start(bf16[64,512]{1,0:T(8,128)(2,1)S(1)} %collective-permute-done.6), channel_id=1, source_target_pairs={{0,1},{1,2},{2,3},{3,4},{4,5},{5,6},{6,7},{7,8},{8,9},{9,10},{10,1... | collective-permute-start | bytes 196616 | tf_op jit(solution)/shard_map/ppermute | solution.py:23
  45.3 9.4 %collective-permute-start.11 = (bf16[64,512]{1,0:T(8,128)(2,1)S(1)}, bf16[64,512]{1,0:T(8,128)(2,1)S(1)}, u32[]{:S(2)}, u32[]{:S(2)}) collective-permute-start(bf16[64,512]{1,0:T(8,128)(2,1)S(1)} %collective-permute-done.9), channel_id=1, source_target_pairs={{0,15},{1,0},{2,1},{3,2},{4,3},{5,4},{6,5},{7,6},{8,7},{9,8},{10,9... | collective-permute-start | bytes 196616 | tf_op jit(solution)/shard_map/ppermute | solution.py:28
  53.7 7.6 %collective-permute-start.10 = (bf16[64,512]{1,0:T(8,128)(2,1)S(1)}, bf16[64,512]{1,0:T(8,128)(2,1)S(1)}, u32[]{:S(2)}, u32[]{:S(2)}) collective-permute-start(bf16[64,512]{1,0:T(8,128)(2,1)S(1)} %collective-permute-done.8), channel_id=1, source_target_pairs={{0,1},{1,2},{2,3},{3,4},{4,5},{5,6},{6,7},{7,8},{8,9},{9,10},{10,1... | collective-permute-start | bytes 196616 | tf_op jit(solution)/shard_map/ppermute | solution.py:23
  54.7 14.1 %collective-permute-start.13 = (bf16[64,512]{1,0:T(8,128)(2,1)S(1)}, bf16[64,512]{1,0:T(8,128)(2,1)S(1)}, u32[]{:S(2)}, u32[]{:S(2)}) collective-permute-start(bf16[64,512]{1,0:T(8,128)(2,1)S(1)} %collective-permute-done.11), channel_id=1, source_target_pairs={{0,15},{1,0},{2,1},{3,2},{4,3},{5,4},{6,5},{7,6},{8,7},{9,8},{10,9... | collective-permute-start | bytes 196616 | tf_op jit(solution)/shard_map/ppermute | solution.py:28
  61.2 7.6 %collective-permute-start.12 = (bf16[64,512]{1,0:T(8,128)(2,1)S(1)}, bf16[64,512]{1,0:T(8,128)(2,1)S(1)}, u32[]{:S(2)}, u32[]{:S(2)}) collective-permute-start(bf16[64,512]{1,0:T(8,128)(2,1)S(1)} %collective-permute-done.10), channel_id=1, source_target_pairs={{0,1},{1,2},{2,3},{3,4},{4,5},{5,6},{6,7},{7,8},{8,9},{9,10},{10,1... | collective-permute-start | bytes 196616 | tf_op jit(solution)/shard_map/ppermute | solution.py:23
  68.8 7.6 %collective-permute-start.14 = (bf16[64,512]{1,0:T(8,128)(2,1)S(1)}, bf16[64,512]{1,0:T(8,128)(2,1)S(1)}, u32[]{:S(2)}, u32[]{:S(2)}) collective-permute-start(bf16[64,512]{1,0:T(8,128)(2,1)S(1)} %collective-permute-done.12), channel_id=1, source_target_pairs={{0,1},{1,2},{2,3},{3,4},{4,5},{5,6},{6,7},{7,8},{8,9},{9,10},{10,1... | collective-permute-start | bytes 196616 | tf_op jit(solution)/shard_map/ppermute | solution.py:23
  105.9 78.9 %copy-start.1 = (f32[1024,128]{1,0:T(8,128)S(1)}, f32[1024,128]{1,0:T(8,128)}, u32[]{:S(2)}) copy-start(f32[1024,128]{1,0:T(8,128)} %param.13) | copy-start | bytes 1572868
Sparse Core Ops, SparseCore 0:
  9.5 48.2 all-gather.1
  106.0 78.7 all-reduce.1
